TPU v7x, 32 devices: a whole 2x2x4 slice. The times are simulated.
32 devices in a mesh: seq: 8 (over z, y), exp: 4 (over x, core).
Axes of the slice: x: 2, y: 2, z: 4, core: 2. Of those that a mesh axis runs over, the one named last changes fastest.
Arguments:
- hidden: bfloat16 [4, 1024, 2048], P('exp', 'seq'), may hold values from -6 to 6
- lengths: int32 [4, 4], P('exp'), may hold values from 1 to 512, 1024 in all within a row
- attn_gain: float32 [2048], replicated, may hold values from 0 to 10
- w_qkv: bfloat16 [2048, 3, 16, 128], P(None, None, 'seq'), may hold values from -0.125 to 0.125
- w_out: bfloat16 [16, 128, 2048], P('seq'), may hold values from -0.125 to 0.125
- moe_gain: float32 [2048], replicated, may hold values from 0.5 to 1.5
- router: bfloat16 [2048, 16], replicated, may hold values from -8 to 8
- routes: int32 [4, 1024, 6], P('exp', 'seq'), may hold values from 0 to 15, all different within a row; in each aligned block of 128 rows (0 to 127, 128 to 255, ..., all dimensions but the last counted through in order) at most 56 rows name the same one
- w_gate_up: bfloat16 [32, 2, 704, 2048], P(('seq', 'exp')), may hold values from -0.125 to 0.125
- w_down: bfloat16 [32, 704, 2048], P(('seq', 'exp')), may hold values from -0.15625 to 0.15625
- final_gain: float32 [2048], replicated, may hold values from 0.5 to 1.5
- lm_head: bfloat16 [102400, 2048], P(('seq', 'exp')), may hold values from -4 to 4
Outputs:
- layer_out: bfloat16 [4, 1024, 2048], P('exp', 'seq')
- logprobs: float32 [16, 102400], P(None, ('seq', 'exp'))
Inputs may be any that keep to these rules, and one draw needn't show every extreme that they name: `routes`: in the rows of one device no expert is named by more than 56 rows; in some devices one expert is named by exactly 56 rows. `lengths`: each row sums to 1024; its largest entry is 512.
All inputs are finite; a program needn't handle non-finite values.
Results may differ from a plain program's by a relative error of at most 0.0095.
The roundings to bfloat16 on the way count: a program that leaves them out, or rounds other values in their place, can miss the bound.
Values may be sent and summed in bfloat16 or wider, within the bound.
No kernel may reach another device: no remote copies, remote signals or barrier semaphores. Data moves between devices by JAX's collectives and lax.ppermute only.
A program may use at most 128 MiB of HBM per device.

v0:
```python
import jax
import jax.numpy as jnp
from jax import lax
from jax.sharding import PartitionSpec as P

epsilon = 1e-06


def joined(value, axis, join):
    pieces = jax.tree.map(lambda part: lax.all_gather(part, axis), value)
    head = jax.tree.map(lambda part: part[0], pieces)
    tail = jax.tree.map(lambda part: part[1:], pieces)
    subtotal, _ = lax.scan(lambda subtotal, piece: (join(subtotal, piece), None), head, tail)
    return subtotal


def rms_scale(values, gain):
    widened = values.astype(jnp.float32)
    inverse = lax.rsqrt(jnp.mean(widened * widened, axis=-1, keepdims=True) + epsilon)
    return widened * inverse * gain


def segment_layout(prompt_lengths, count):
    ends = jnp.cumsum(prompt_lengths)
    starts = ends - prompt_lengths
    places = jnp.arange(count, dtype=jnp.int32)
    member = ((places[:, None] >= starts[None, :]) & (places[:, None] < ends[None, :])).astype(
        jnp.int32
    )
    numbers = jnp.arange(prompt_lengths.shape[0], dtype=jnp.int32)
    segment = jnp.sum(member * numbers[None, :], axis=1)
    offset = places - jnp.sum(member * starts[None, :], axis=1)
    return (segment, offset)


def rotary(values, positions):
    half_size = values.shape[-1] // 2
    freqs = 10000.0 ** (-2.0 * jnp.arange(half_size, dtype=jnp.float32) / values.shape[-1])
    angles = positions.astype(jnp.float32)[:, None] * freqs[None, :]
    cosine = jnp.cos(angles)[:, None, :]
    sine = jnp.sin(angles)[:, None, :]
    first_half = values[..., :half_size]
    second_half = values[..., half_size:]
    return jnp.concatenate(
        [first_half * cosine - second_half * sine, second_half * cosine + first_half * sine],
        axis=-1,
    )


def pair_swap(value):
    count = lax.axis_size("exp")
    return lax.ppermute(value, "exp", [(i, i ^ 1) for i in range(count)])


def merge_softmax(earlier, later):
    highest = jnp.maximum(earlier[0], later[0])
    return (
        highest,
        earlier[1] * jnp.exp(earlier[0] - highest) + later[1] * jnp.exp(later[0] - highest),
    )


def per_device(
    hidden,
    lengths,
    attn_gain,
    w_qkv,
    w_out,
    moe_gain,
    router,
    routes,
    w_gate_up,
    w_down,
    final_gain,
    lm_head,
):
    seq_count = lax.axis_size("seq")
    group_count = lax.axis_size("exp")
    device_count = seq_count * group_count
    token_rows = hidden[0]
    tok_rows = token_rows.shape[0]
    model_width = token_rows.shape[1]
    group_tokens = tok_rows * seq_count
    head_count = w_qkv.shape[2]
    head_size = w_qkv.shape[3]
    scale_factor = head_size ** (-0.5)
    prompt_lengths = lengths[0]
    segment, offset = segment_layout(prompt_lengths, group_tokens)
    normed = rms_scale(token_rows, attn_gain).astype(jnp.bfloat16)
    qkv_weight = w_qkv.reshape(model_width, 3 * head_count * head_size)
    qkv = jnp.dot(
        lax.all_gather(normed, "seq", axis=0, tiled=True),
        qkv_weight,
        preferred_element_type=jnp.float32,
    ).reshape(group_tokens, 3, head_count, head_size)
    query = rotary(qkv[:, 0], offset).astype(jnp.bfloat16)
    keys = rotary(qkv[:, 1], offset).astype(jnp.bfloat16)
    values = qkv[:, 2].astype(jnp.bfloat16)
    block_rows = min(512, group_tokens)
    key_places = jnp.arange(group_tokens, dtype=jnp.int32)

    def one_block(block_index):
        first_row = block_index * block_rows
        block_query = lax.dynamic_slice_in_dim(query, first_row, block_rows, 0)
        block_segment = lax.dynamic_slice_in_dim(segment, first_row, block_rows, 0)
        query_places = first_row + jnp.arange(block_rows, dtype=jnp.int32)
        scores = (
            jnp.einsum("qhd,khd->hqk", block_query, keys, preferred_element_type=jnp.float32)
            * scale_factor
        )
        allowed = (block_segment[:, None] == segment[None, :]) & (
            key_places[None, :] <= query_places[:, None]
        )
        scores = jnp.where(allowed[None], scores, -1e30)
        highest = jnp.max(scores, axis=2, keepdims=True)
        weights = jnp.exp(scores - highest)
        probs = (weights / jnp.sum(weights, axis=2, keepdims=True)).astype(jnp.bfloat16)
        return jnp.einsum("hqk,khd->qhd", probs, values, preferred_element_type=jnp.float32).astype(
            jnp.bfloat16
        )

    blocks = lax.map(one_block, jnp.arange(group_tokens // block_rows, dtype=jnp.int32))
    heads_flat = blocks.reshape(group_tokens, head_count * head_size)
    regrouped = lax.all_to_all(heads_flat, "seq", split_axis=0, concat_axis=1, tiled=True)
    core = lax.axis_index("exp") % 2
    half_size = head_size // 2
    own_half = lax.dynamic_slice_in_dim(w_out, core * half_size, half_size, axis=1)
    own_weight = lax.all_gather(own_half, "seq", axis=0, tiled=True)
    other_weight = pair_swap(own_weight)
    regrouped = regrouped.reshape(tok_rows, -1, head_size)
    own_heads = lax.dynamic_slice_in_dim(regrouped, core * half_size, half_size, axis=2)
    other_heads = lax.dynamic_slice_in_dim(regrouped, (1 - core) * half_size, half_size, axis=2)
    mixed = jnp.einsum(
        "thd,hdo->to", own_heads, own_weight, preferred_element_type=jnp.float32
    ) + jnp.einsum("thd,hdo->to", other_heads, other_weight, preferred_element_type=jnp.float32)
    middle = (token_rows.astype(jnp.float32) + mixed).astype(jnp.bfloat16)
    expert_in = rms_scale(middle, moe_gain).astype(jnp.bfloat16)
    logits = jnp.dot(expert_in, router, preferred_element_type=jnp.float32)
    expert_count = router.shape[1]
    token_routes = routes[0]
    top_count = token_routes.shape[1]
    expert_ids = jnp.arange(expert_count, dtype=jnp.int32)
    chosen_mask = token_routes[:, :, None] == expert_ids[None, None, :]
    chosen = jnp.sum(jnp.where(chosen_mask, logits[:, None, :], 0.0), axis=2)
    gates = jax.nn.softmax(chosen, axis=-1)
    capacity = max(2, tok_rows * top_count * 7 // (6 * expert_count))
    flat_mask = chosen_mask.reshape(tok_rows * top_count, expert_count).astype(jnp.int32)
    earlier_count = jnp.cumsum(flat_mask, axis=0) - flat_mask
    slot_index = jnp.sum(earlier_count * flat_mask, axis=1)
    target = (token_routes.reshape(-1) * capacity + slot_index).reshape(tok_rows, top_count)
    slot_total = expert_count * capacity
    placed = target[:, :, None] == jnp.arange(slot_total, dtype=jnp.int32)[None, None, :]
    dispatch_table = jnp.any(placed, axis=1).astype(jnp.bfloat16)
    slot_weights = jnp.sum(jnp.where(placed, gates[:, :, None], 0.0), axis=1)
    packed = lax.dot_general(
        dispatch_table, expert_in, (((0,), (0,)), ((), ())), preferred_element_type=jnp.float32
    ).astype(jnp.bfloat16)
    shares = device_count // expert_count
    assert capacity % shares == 0
    outgoing = packed.reshape(device_count, capacity // shares, model_width)
    gate_up = w_gate_up[0]
    down_weight = w_down[0]
    other_gate_up = pair_swap(gate_up)
    other_down = pair_swap(down_weight)
    arrived = lax.all_to_all(outgoing, ("seq", "exp"), split_axis=0, concat_axis=0, tiled=True)
    arrived_shape = arrived.shape
    flat_rows = arrived.reshape(-1, model_width)

    def share_part(pair, down):
        both = jnp.einsum("rd,gfd->rgf", flat_rows, pair, preferred_element_type=jnp.float32)
        act = (jax.nn.silu(both[:, 0]) * both[:, 1]).astype(jnp.bfloat16)
        part = jnp.dot(act, down, preferred_element_type=jnp.float32).astype(jnp.bfloat16)
        return part.astype(jnp.float32)

    part_sum = share_part(gate_up, down_weight) + share_part(other_gate_up, other_down)
    returned = lax.all_to_all(
        part_sum.astype(jnp.bfloat16).reshape(arrived_shape),
        ("seq", "exp"),
        split_axis=0,
        concat_axis=0,
        tiled=True,
    )
    summed = returned.reshape(slot_total, model_width).astype(jnp.float32)
    routed = jnp.dot(
        slot_weights, summed, precision=lax.Precision.HIGHEST, preferred_element_type=jnp.float32
    )
    layer_rows = (middle.astype(jnp.float32) + routed).astype(jnp.bfloat16)
    prompt_count = prompt_lengths.shape[0]
    last_places = jnp.cumsum(prompt_lengths) - 1
    here_places = lax.axis_index("seq") * tok_rows + jnp.arange(tok_rows, dtype=jnp.int32)
    select_table = (last_places[:, None] == here_places[None, :]).astype(jnp.bfloat16)
    picked = jnp.dot(select_table, layer_rows, preferred_element_type=jnp.float32)
    board = jnp.zeros((group_count * prompt_count, model_width), jnp.bfloat16)
    board = lax.dynamic_update_slice_in_dim(
        board, picked.astype(jnp.bfloat16), lax.axis_index("exp") * prompt_count, 0
    )
    last_rows = lax.psum(board, ("seq", "exp")).astype(jnp.float32)
    final = rms_scale(last_rows, final_gain).astype(jnp.bfloat16)
    vocab_scores = lax.dot_general(
        final, lm_head, (((1,), (1,)), ((), ())), preferred_element_type=jnp.float32
    )
    local_peak = jnp.max(vocab_scores, axis=1)
    local_total = jnp.sum(jnp.exp(vocab_scores - local_peak[:, None]), axis=1)
    global_peak, global_total = joined((local_peak, local_total), ("seq", "exp"), merge_softmax)
    logprobs = vocab_scores - (global_peak + jnp.log(global_total))[:, None]
    return (layer_rows[None], logprobs)


def solution(mesh):
    return jax.shard_map(
        per_device,
        mesh=mesh,
        in_specs=(
            P("exp", "seq", None),
            P("exp", None),
            P(),
            P(None, None, "seq", None),
            P("seq", None, None),
            P(),
            P(),
            P("exp", "seq", None),
            P(("seq", "exp"), None, None, None),
            P(("seq", "exp"), None, None),
            P(),
            P(("seq", "exp"), None),
        ),
        out_specs=(P("exp", "seq", None), P(None, ("seq", "exp"))),
        check_vma=False,
    )
```

profile of v0, /device:TPU:0, one launch (start us, length us, event | category | flops | bytes accessed | tf_op | source)
XLA Modules:
  0.0 637.5 jit_solution(17529622819611426284)
XLA Ops:
  7.2 1.3 fusion.48
  8.6 2.1 fusion.50
  10.7 0.8 constant_dynamic-slice_fusion.2
  11.8 8.0 %reshape.269 = bf16[2048,768]{1,0:T(8,128)(2,1)} reshape(bf16[2048,3,2,128]{3,2,1,0:T(2,128)(2,1)} %param.19) | data formatting | bytes 6291456 | tf_op jit(solution)/shard_map/reshape | solution.py:90
  19.8 4.8 copy.43
  24.7 1.0 multiply_cosine_fusion
  25.7 61.2 %all-gather.5.cloned.1.call-done = bf16[1024,2048]{1,0:T(8,128)(2,1)} async-done(((bf16[128,2048]{1,0:T(8,128)(2,1)}), bf16[1024,2048]{1,0:T(8,128)(2,1)}) %all-gather.5.cloned.1.call-update) | async-done | bytes 4194320 | tf_op jit(solution)/shard_map/all_gather | solution.py:92
  86.9 6.2 fusion.31
  93.6 1.2 copy-done.4
  95.2 1.4 fusion.51
  96.8 64.4 %all-gather.7.cloned.1.call-done = bf16[16,64,2048]{2,1,0:T(8,128)(2,1)} async-done(((bf16[2,64,2048]{2,1,0:T(8,128)(2,1)}), bf16[16,64,2048]{2,1,0:T(8,128)(2,1)}) %all-gather.7.cloned.1.call-update) | async-done | bytes 4194320 | tf_op jit(solution)/shard_map/all_gather | solution.py:128
  161.3 17.8 %while.24 = (s32[]{:T(128)}, bf16[2,512,2,128]{3,2,1,0:T(2,128)(2,1)S(1)}, s32[2]{0:T(128)S(1)}, s32[1024]{0:T(1024)S(1)}, bf16[1024,2,128]{0,2,1:T(8,128)(2,1)S...) while((s32[]{:T(128)}, ...), condition=%wide.region_7.8_spmd.clone, body=%wide.region_4.7_spmd.clone.sunk | while | flops 544867840 | bytes 11557047 | solution.py:122
  161.3 0.6 dynamic_slice.72
  162.6 0.6 fusion.116
  163.2 3.7 fusion.117
  166.9 2.9 fusion.118
  170.2 0.6 dynamic_slice.72
  171.5 0.6 fusion.116
  172.1 3.7 fusion.117
  175.8 2.9 fusion.118
  179.1 1.1 all_to_all.18
  180.2 3.7 all-to-all-start
  184.3 1.7 reduce-window.11
  186.7 0.5 fusion.33
  187.1 12.0 %all-to-all-done = bf16[8,128,256]{2,1,0:T(8,128)(2,1)S(1)} async-done(((bf16[8,128,256]{2,1,0:T(8,128)(2,1)}), bf16[8,128,256]{2,1,0:T(8,128)(2,1)S(1)}, u32[]{:S(2)}, u32[]{:S(2)}) %all-to-all-start) | async-done | bytes 524320 | tf_op jit(solution)/shard_map/all_to_all | solution.py:124
  199.4 2.9 convolution_bitcast_fusion.1
  202.4 3.1 multiply_reduce_fusion
  205.5 3.0 convolution_convert_fusion
  208.5 5.8 reshape.272
  214.3 3.7 all-to-all-start.1
  218.6 93.3 %all-to-all-done.1 = bf16[32,28,2048]{2,1,0:T(8,128)(2,1)} async-done(((bf16[32,28,2048]{2,1,0:T(8,128)(2,1)}), bf16[32,28,2048]{2,1,0:T(8,128)(2,1)}, u32[]{:S(2)}, u32[]{:S(2)}) %all-to-all-start.1) | async-done | bytes 3670048 | tf_op jit(solution)/shard_map/all_to_all | solution.py:165
  311.9 5.9 reshape.292
  317.8 9.4 %fusion.76 = f32[896,2,704]{0,2,1:T(8,128)S(1)} fusion(bf16[896,2048,1]{1,0,2:T(8,128)(2,1)} %reshape.292, bf16[1,2,704,2048]{3,2,1,0:T(8,128)(2,1)} %param.24), kind=kOutput, calls=%fused_computation.127 | convolution fusion | flops 5167382528 | bytes 14483456 | tf_op jit(solution)/shard_map/rd,gfd->rgf/dot_general | solution.py:170
  327.3 3.4 fusion.44
  330.7 8.4 %fusion.88 = f32[896,2,704]{0,2,1:T(8,128)S(1)} fusion(bf16[896,2048,1]{1,0,2:T(8,128)(2,1)S(1)} %copy-done.3, bf16[2,704,2048]{2,1,0:T(8,128)(2,1)} %collective-permute-done.1), kind=kOutput, calls=%fused_computation.134 | convolution fusion | flops 5167382528 | bytes 14483456 | tf_op jit(solution)/shard_map/rd,gfd->rgf/dot_general | solution.py:170
  339.2 6.9 %add_convert_fusion = bf16[896,2048]{1,0:T(8,128)(2,1)} fusion(bf16[896,2048]{1,0:T(8,128)(2,1)S(1)} %fusion.44, bf16[704,2048]{1,0:T(8,128)(2,1)} %collective-permute-done.2, f32[896,2,704]{0,2,1:T(8,128)S(1)} %fusion.88), kind=kOutput, calls=%fused_computation.31 | convolution fusion | flops 2596651008 | bytes 15269888 | tf_op jit(solution)/shard_map/dot_general | solution.py:172
  346.0 5.8 reshape.274
  351.9 4.1 all-to-all-start.2
  357.1 92.8 %all-to-all-done.2 = bf16[32,28,2048]{2,1,0:T(8,128)(2,1)} async-done(((bf16[32,28,2048]{2,1,0:T(8,128)(2,1)}), bf16[32,28,2048]{2,1,0:T(8,128)(2,1)}, u32[]{:S(2)}, u32[]{:S(2)}) %all-to-all-start.2) | async-done | bytes 3670048 | tf_op jit(solution)/shard_map/all_to_all | solution.py:176
  449.8 5.8 reshape.275
  455.7 3.9 fusion.40
  459.8 0.6 copy-done.6
  460.5 117.0 %all-reduce.5.cloned.1.call-done = bf16[16,2048]{1,0:T(8,128)(2,1)} async-done(((bf16[16,2048]{1,0:T(8,128)(2,1)}), bf16[16,2048]{1,0:T(8,128)(2,1)}) %all-reduce.5.cloned.1.call-update) | async-done | bytes 65552 | tf_op jit(solution)/shard_map/psum | solution.py:197
  577.5 1.0 fusion.54
  578.5 8.5 %fusion.87 = (f32[16]{0:T(128)S(1)}, f32[16,3200]{1,0:T(8,128)S(1)}) fusion(bf16[3200,2048]{1,0:T(8,128)(2,1)} %param.27, bf16[16,2048]{1,0:T(8,128)(2,1)} %all-reduce.5.cloned.1.call-done, f32[2048]{0:T(1024)S(1)} %copy-done.10, f32[16]{0:T(128)S(1)} %add_rsqrt_fusion), kind=kOutput, calls=%fused_computation.133 | convolution fusion | flops 209897456 | bytes 13385856 | tf_op jit(solution)/shard_map/dot_general | solution.py:199
  587.7 40.8 %all-reduce.2 = (f32[512]{0:T(512)S(1)}, f32[512]{0:T(512)S(1)}) all-reduce(f32[512]{0:T(512)S(1)} %dynamic-update-slice, f32[512]{0:T(512)S(1)} %dynamic-update-slice.1), channel_id=2, replica_groups=mesh['seq'=8,'exp'=4] {'seq','exp'}, use_global_device_ids=true, to_apply=%add | all-reduce | flops 1024 | bytes 8192
  628.8 1.3 while.23
  630.2 0.8 broadcast_subtract_fusion
  (122 shorter events, 7.4 us)
Async XLA Ops:
  7.2 3.5 copy-start
  7.2 4.4 copy-start.12
  7.2 79.7 %all-gather.5.cloned.1.call-start = ((), (), s32[]{:S(2)}) async-start(), calls=%async_computation.3 | async-start | bytes 4718592 | tf_op jit(solution)/shard_map/all_gather | solution.py:92
  10.6 150.7 %all-gather.7.cloned.1.call-start = ((), (), s32[]{:S(2)}) async-start(), calls=%async_computation.4 | async-start | bytes 4718592 | tf_op jit(solution)/shard_map/all_gather | solution.py:128
  93.1 1.7 copy-start.4
  161.3 41.1 %collective-permute-start = (bf16[16,64,2048]{2,1,0:T(8,128)(2,1)}, bf16[16,64,2048]{2,1,0:T(8,128)(2,1)}, u32[]{:S(2)}, u32[]{:S(2)}) collective-permute-start(bf16[16,64,2048]{2,1,0:T(8,128)(2,1)} %all-gather.7.cloned.1.call-done), channel_id=1, source_target_pairs={{0,1},{1,0},{2,3},{3,2},{4,5},{5,4},{6,7},{7,6},{8,9},{9,8},{10,11... | collective-permute-start | bytes 12582920 | tf_op jit(solution)/shard_map/ppermute | solution.py:52
  161.3 22.6 %copy-start.9 = (s32[1,128,6]{1,0,2:T(1,128)S(1)}, s32[1,128,6]{1,0,2:T(1,128)}, u32[]{:S(2)}) copy-start(s32[1,128,6]{1,0,2:T(1,128)} %param.23) | copy-start | bytes 9220
  180.2 18.9 %all-to-all-start = ((bf16[8,128,256]{2,1,0:T(8,128)(2,1)}), bf16[8,128,256]{2,1,0:T(8,128)(2,1)S(1)}, u32[]{:S(2)}, u32[]{:S(2)}) async-start(bf16[8,128,256]{2,1,0:T(8,128)(2,1)} %all_to_all.18), calls=%async_computation | async-start | bytes 1048576 | tf_op jit(solution)/shard_map/all_to_all | solution.py:124
  184.2 18.2 %copy-start.2 = (bf16[1,128,2048]{2,1,0:T(8,128)(2,1)S(1)}, bf16[1,128,2048]{2,1,0:T(8,128)(2,1)}, u32[]{:S(2)}) copy-start(bf16[1,128,2048]{2,1,0:T(8,128)(2,1)} %param.16) | copy-start | bytes 1572868
  202.4 3.1 copy-start.8
  214.3 97.6 %all-to-all-start.1 = ((bf16[32,28,2048]{2,1,0:T(8,128)(2,1)}), bf16[32,28,2048]{2,1,0:T(8,128)(2,1)}, u32[]{:S(2)}, u32[]{:S(2)}) async-start(bf16[32,28,2048]{2,1,0:T(8,128)(2,1)} %reshape.272), calls=%async_computation.1 | async-start | bytes 8388608 | tf_op jit(solution)/shard_map/all_to_all | solution.py:165
  218.1 112.7 %collective-permute-start.1 = (bf16[2,704,2048]{2,1,0:T(8,128)(2,1)}, bf16[2,704,2048]{2,1,0:T(8,128)(2,1)}, u32[]{:S(2)}, u32[]{:S(2)}) collective-permute-start(bf16[2,704,2048]{2,1,0:T(8,128)(2,1)} %bitcast.143), channel_id=1, source_target_pairs={{0,1},{1,0},{2,3},{3,2},{4,5},{5,4},{6,7},{7,6},{8,9},{9,8},{10,11... | collective-permute-start | bytes 17301512 | tf_op jit(solution)/shard_map/ppermute | solution.py:52
  218.3 120.9 %collective-permute-start.2 = (bf16[704,2048]{1,0:T(8,128)(2,1)}, bf16[704,2048]{1,0:T(8,128)(2,1)}, u32[]{:S(2)}, u32[]{:S(2)}) collective-permute-start(bf16[704,2048]{1,0:T(8,128)(2,1)} %bitcast.144), channel_id=1, source_target_pairs={{0,1},{1,0},{2,3},{3,2},{4,5},{5,4},{6,7},{7,6},{8,9},{9,8},{10,11... | collective-permute-start | bytes 8650760 | tf_op jit(solution)/shard_map/ppermute | solution.py:52
  317.8 9.4 %copy-start.11 = (bf16[1,704,2048]{2,1,0:T(8,128)(2,1)S(1)}, bf16[1,704,2048]{2,1,0:T(8,128)(2,1)}, u32[]{:S(2)}) copy-start(bf16[1,704,2048]{2,1,0:T(8,128)(2,1)} %param.25) | copy-start | bytes 8650756
  327.3 3.4 copy-start.3
  351.9 4.4 copy-start.7
  351.9 98.0 %all-to-all-start.2 = ((bf16[32,28,2048]{2,1,0:T(8,128)(2,1)}), bf16[32,28,2048]{2,1,0:T(8,128)(2,1)}, u32[]{:S(2)}, u32[]{:S(2)}) async-start(bf16[32,28,2048]{2,1,0:T(8,128)(2,1)} %reshape.274), calls=%async_computation.2 | async-start | bytes 8388608 | tf_op jit(solution)/shard_map/all_to_all | solution.py:176
  356.0 221.6 %all-reduce.5.cloned.1.call-start = ((), (), s32[]{:S(2)}) async-start(), calls=%async_computation.5 | async-start | bytes 131072 | tf_op jit(solution)/shard_map/psum | solution.py:197
  455.7 122.8 %copy-start.10 = (f32[2048]{0:T(1024)S(1)}, f32[2048]{0:T(1024)}, u32[]{:S(2)}) copy-start(f32[2048]{0:T(1024)} %param.26) | copy-start | bytes 24580
  459.6 127.4 %copy-start.5 = (bf16[128,2048]{1,0:T(8,128)(2,1)}, bf16[128,2048]{1,0:T(8,128)(2,1)S(1)}, u32[]{:S(2)}) copy-start(bf16[128,2048]{1,0:T(8,128)(2,1)S(1)} %fusion.40) | copy-start | bytes 1572868
  459.8 0.6 copy-start.6
  578.5 52.4 %copy-start.1 = (bf16[2,128,2048]{2,1,0:T(8,128)(2,1)S(1)}, bf16[2,128,2048]{2,1,0:T(8,128)(2,1)}, u32[]{:S(2)}) copy-start(bf16[2,128,2048]{2,1,0:T(8,128)(2,1)} %param.20) | copy-start | bytes 3145732
Sparse Core Ops, SparseCore 0:
  10.7 76.0 all-gather.4
  89.6 71.6 all-gather.6
  460.6 116.8 all-reduce.4
where the time goes:
time: 639 us; the launch traced here: 637 us
  waiting for transfers between devices  441 us (69%)
  matrix products  69.6 us (11%)
  local copies, waits for them, and re-layouts  45.9 us (7%)
  blocking collectives  40.8 us (6%)
  between operations  14.3 us (2%)
  starting transfers between devices  12.4 us (2%)
  other arithmetic  11.9 us (2%)
    psum x1, waiting for transfers between devices, per_device(): last_rows = lax.psum(board, ('seq', 'exp')).astype(jnp.float32)  117 us
    all_to_all x1, waiting for transfers between devices, per_device(): lax.all_to_all(outgoing, ('seq', 'exp'), split_axis=0, concat_axis=0, til...  93.3 us
    all_to_all x1, waiting for transfers between devices, per_device(): lax.all_to_all(part_sum.astype(jnp.bfloat16).reshape(arrived_shape), ('se...  92.8 us
    all_gather x1, waiting for transfers between devices, per_device(): own_weight = lax.all_gather(own_half, 'seq', axis=0, tiled=True)  64.4 us
    all_gather x1, waiting for transfers between devices, per_device(): lax.all_gather(normed, 'seq', axis=0, tiled=True)  61.2 us
    unnamed x1, blocking collectives  40.8 us
    dot_general x2, matrix products, share_part(): jnp.einsum('rd,gfd->rgf', flat_rows, pair, preferred_element_type=jnp.flo...  17.8 us
  transfers between devices with their start and end apart: 9, of which 6 were waited for; matrix products, arithmetic and copies ran while one was open for 12% of the time, Pallas kernels for 0%

commit v1 on v0

--- a/solution.py
+++ b/solution.py
@@ -4,6 +4,14 @@
 from jax.sharding import PartitionSpec as P
 
 epsilon = 1e-06
+
+
+def arrange_desk(sample, along_dim):
+    sample = jnp.moveaxis(sample, 0, along_dim)
+    h_now = sample.shape
+    return sample.reshape(
+        *h_now[:along_dim], h_now[along_dim] * h_now[along_dim + 1], *h_now[along_dim + 2 :]
+    )
 
 
 def joined(value, axis, join):
@@ -125,7 +133,19 @@
     core = lax.axis_index("exp") % 2
     half_size = head_size // 2
     own_half = lax.dynamic_slice_in_dim(w_out, core * half_size, half_size, axis=1)
-    own_weight = lax.all_gather(own_half, "seq", axis=0, tiled=True)
+    parts_n = jax.lax.axis_size("seq")
+    crops = [(rr, (rr + 1) % parts_n) for rr in range(parts_n)]
+    leaves = [(nth, to_i) for to_i, nth in crops]
+    view_out, part_now = ([], [])
+    for i0 in range(parts_n - 1):
+        if i0 % 2 == 0:
+            view_out.append(jax.lax.ppermute(view_out[-1] if view_out else own_half, "seq", crops))
+        else:
+            part_now.append(jax.lax.ppermute(part_now[-1] if part_now else own_half, "seq", leaves))
+    found_now = jnp.stack([*view_out[::-1], own_half, *part_now], 0)
+    carry_in = jax.lax.axis_index("seq") - len(view_out)
+    found_now = found_now[(jnp.arange(parts_n) - carry_in) % parts_n]
+    own_weight = arrange_desk(found_now, 0)
     other_weight = pair_swap(own_weight)
     regrouped = regrouped.reshape(tok_rows, -1, head_size)
     own_heads = lax.dynamic_slice_in_dim(regrouped, core * half_size, half_size, axis=2)

time: 639 us -> 627 us (0.981)
  waiting for transfers between devices: 441 us -> 377 us
  starting transfers between devices: 12.4 us -> 53.7 us
  local copies, waits for them, and re-layouts: 45.9 us -> 57.6 us
    all_gather x1 -> x0, waiting for transfers between devices: 64.4 us -> none  [per_device(): own_weight = lax.all_gather(own_half, 'seq', axis=0, tiled=True)]
    ppermute x0 -> x7, waiting for transfers between devices: none -> 62.1 us  [the longest x4 62.1 us: per_device(): jax.lax.ppermute(view_out[-1] if view_out else own_half, 'seq', crops)]
    all_gather x1, waiting for transfers between devices: 61.2 us -> 0.01 us  [per_device(): lax.all_gather(normed, 'seq', axis=0, tiled=True)]
    ppermute x0 -> x7, starting transfers between devices: none -> 38.8 us  [the longest x3 33.3 us: per_device(): jax.lax.ppermute(part_now[-1] if part_now else own_half, 'seq', leaves)]
    unnamed x33 -> x44, local copies, waits for them, and re-layouts: 2.96 us -> 12 us
  transfers between devices with their start and end apart: 9 -> 15, of which waited for: 6 -> 8; matrix products, arithmetic and copies ran while one was open for 12% -> 13% of each run, Pallas kernels for 0% -> 0%
where the time goes in v1:
time: 627 us; the launch traced here: 625 us
  waiting for transfers between devices  377 us (60%)
  matrix products  66.4 us (11%)
  local copies, waits for them, and re-layouts  57.6 us (9%)
  starting transfers between devices  53.7 us (9%)
  blocking collectives  40.8 us (7%)
  between operations  14.6 us (2%)
  other arithmetic  13.2 us (2%)
    psum x1, waiting for transfers between devices, per_device(): last_rows = lax.psum(board, ('seq', 'exp')).astype(jnp.float32)  117 us
    all_to_all x1, waiting for transfers between devices, per_device(): lax.all_to_all(outgoing, ('seq', 'exp'), split_axis=0, concat_axis=0, til...  93.3 us
    all_to_all x1, waiting for transfers between devices, per_device(): lax.all_to_all(part_sum.astype(jnp.bfloat16).reshape(arrived_shape), ('se...  92.8 us
    ppermute x4, waiting for transfers between devices, per_device(): jax.lax.ppermute(view_out[-1] if view_out else own_half, 'seq', crops)  62.1 us
    unnamed x1, blocking collectives  40.8 us
    ppermute x3, starting transfers between devices, per_device(): jax.lax.ppermute(part_now[-1] if part_now else own_half, 'seq', leaves)  33.3 us
    dot_general x2, matrix products, share_part(): jnp.einsum('rd,gfd->rgf', flat_rows, pair, preferred_element_type=jnp.flo...  17.8 us
  transfers between devices with their start and end apart: 15, of which 8 were waited for; matrix products, arithmetic and copies ran while one was open for 13% of the time, Pallas kernels for 0%

profile of v1, /device:TPU:0, one launch (start us, length us, event | category | flops | bytes accessed | tf_op | source)
XLA Modules:
  0.0 625.3 jit_solution(1628489898753885138)
XLA Ops:
  7.2 1.2 fusion.48
  8.5 2.0 fusion.50
  10.5 1.9 constant_dynamic-slice_fusion.2
  12.4 3.0 collective-permute-start
  15.4 19.5 %collective-permute-done = bf16[2,64,2048]{2,1,0:T(8,128)(2,1)} collective-permute-done((bf16[2,64,2048]{2,1,0:T(8,128)(2,1)}, bf16[2,64,2048]{2,1,0:T(8,128)(2,1)}, u32[]{:S(2)}, u32[]{:S(2)}) %collective-permute-start) | collective-permute-done | bytes 524320 | tf_op jit(solution)/shard_map/ppermute | solution.py:142
  35.0 4.6 collective-permute-start.4
  40.4 6.8 %reshape.321 = bf16[2048,768]{1,0:T(8,128)(2,1)S(1)} reshape(bf16[2048,3,2,128]{3,2,1,0:T(2,128)(2,1)} %param.19) | data formatting | bytes 6291456 | tf_op jit(solution)/shard_map/reshape | solution.py:98
  47.2 3.0 copy.32
  50.2 8.6 %collective-permute-done.1 = bf16[2,64,2048]{2,1,0:T(8,128)(2,1)} collective-permute-done((bf16[2,64,2048]{2,1,0:T(8,128)(2,1)}, bf16[2,64,2048]{2,1,0:T(8,128)(2,1)}, u32[]{:S(2)}, u32[]{:S(2)}) %collective-permute-start.1) | collective-permute-done | bytes 524320 | tf_op jit(solution)/shard_map/ppermute | solution.py:142
  59.0 11.4 %collective-permute-start.5 = (bf16[2,64,2048]{2,1,0:T(8,128)(2,1)}, bf16[2,64,2048]{2,1,0:T(8,128)(2,1)S(1)}, u32[]{:S(2)}, u32[]{:S(2)}) collective-permute-start(bf16[2,64,2048]{2,1,0:T(8,128)(2,1)} %collective-permute-done.4), channel_id=1, source_target_pairs={{4,0},{8,4},{12,8},{16,12},{20,16},{24,20},{28,24},{0,28},{5,1},{9... | collective-permute-start | bytes 1572872 | tf_op jit(solution)/shard_map/ppermute | solution.py:144
  70.4 22.2 %collective-permute-done.2 = bf16[2,64,2048]{2,1,0:T(8,128)(2,1)S(1)} collective-permute-done((bf16[2,64,2048]{2,1,0:T(8,128)(2,1)}, bf16[2,64,2048]{2,1,0:T(8,128)(2,1)S(1)}, u32[]{:S(2)}, u32[]{:S(2)}) %collective-permute-start.2) | collective-permute-done | bytes 524320 | tf_op jit(solution)/shard_map/ppermute | solution.py:142
  92.5 2.4 collective-permute-start.3
  94.9 1.8 multiply_cosine_fusion
  96.7 17.4 %collective-permute-start.6 = (bf16[2,64,2048]{2,1,0:T(8,128)(2,1)S(1)}, bf16[2,64,2048]{2,1,0:T(8,128)(2,1)S(1)}, u32[]{:S(2)}, u32[]{:S(2)}) collective-permute-start(bf16[2,64,2048]{2,1,0:T(8,128)(2,1)S(1)} %collective-permute-done.5), channel_id=1, source_target_pairs={{4,0},{8,4},{12,8},{16,12},{20,16},{24,20},{28,24},{0,28},{5,1},{9... | collective-permute-start | bytes 1572872 | tf_op jit(solution)/shard_map/ppermute | solution.py:144
  114.0 11.8 %collective-permute-done.3 = bf16[2,64,2048]{2,1,0:T(8,128)(2,1)S(1)} collective-permute-done((bf16[2,64,2048]{2,1,0:T(8,128)(2,1)S(1)}, bf16[2,64,2048]{2,1,0:T(8,128)(2,1)S(1)}, u32[]{:S(2)}, u32[]{:S(2)}) %collective-permute-start.3) | collective-permute-done | bytes 524320 | tf_op jit(solution)/shard_map/ppermute | solution.py:142
  127.6 1.9 bitcast_dynamic-update-slice_fusion.5
  129.5 1.9 bitcast_dynamic-update-slice_fusion.4
  132.3 1.9 bitcast_dynamic-update-slice_fusion.2
  135.9 5.1 gather_fusion
  141.0 5.3 fusion.31
  148.3 17.7 %while.24 = (s32[]{:T(128)}, bf16[2,512,2,128]{3,2,1,0:T(2,128)(2,1)S(1)}, s32[2]{0:T(128)S(1)}, s32[1024]{0:T(1024)S(1)}, bf16[1024,2,128]{0,2,1:T(8,128)(2,1)S...) while((s32[]{:T(128)}, ...), condition=%wide.region_7.8_spmd.clone, body=%wide.region_4.7_spmd.clone.sunk | while | flops 544867840 | bytes 11557047 | solution.py:130
  150.2 3.7 fusion.119
  153.9 2.9 fusion.120
  159.0 3.7 fusion.119
  162.7 2.9 fusion.120
  166.0 1.1 all_to_all.18
  167.1 6.1 all-to-all-start
  173.6 1.7 reduce-window.11
  176.4 12.0 %all-to-all-done = bf16[8,128,256]{2,1,0:T(8,128)(2,1)S(1)} async-done(((bf16[8,128,256]{2,1,0:T(8,128)(2,1)}), bf16[8,128,256]{2,1,0:T(8,128)(2,1)S(1)}, u32[]{:S(2)}, u32[]{:S(2)}) %all-to-all-start) | async-done | bytes 524320 | tf_op jit(solution)/shard_map/all_to_all | solution.py:132
  188.7 3.1 convolution_bitcast_fusion
  193.0 3.0 convolution_convert_fusion
  196.0 5.8 reshape.325
  201.8 3.8 all-to-all-start.1
  206.2 93.3 %all-to-all-done.1 = bf16[32,28,2048]{2,1,0:T(8,128)(2,1)} async-done(((bf16[32,28,2048]{2,1,0:T(8,128)(2,1)}), bf16[32,28,2048]{2,1,0:T(8,128)(2,1)}, u32[]{:S(2)}, u32[]{:S(2)}) %all-to-all-start.1) | async-done | bytes 3670048 | tf_op jit(solution)/shard_map/all_to_all | solution.py:185
  299.5 5.9 reshape.353
  305.5 9.4 %fusion.78 = f32[896,2,704]{0,2,1:T(8,128)S(1)} fusion(bf16[896,2048,1]{1,0,2:T(8,128)(2,1)} %reshape.353, bf16[1,2,704,2048]{3,2,1,0:T(8,128)(2,1)} %param.24), kind=kOutput, calls=%fused_computation.143 | convolution fusion | flops 5167382528 | bytes 14483456 | tf_op jit(solution)/shard_map/rd,gfd->rgf/dot_general | solution.py:190
  314.9 3.4 fusion.44
  318.4 8.4 %fusion.90 = f32[896,2,704]{0,2,1:T(8,128)S(1)} fusion(bf16[896,2048,1]{1,0,2:T(8,128)(2,1)S(1)} %copy-done.3, bf16[2,704,2048]{2,1,0:T(8,128)(2,1)} %collective-permute-done.8), kind=kOutput, calls=%fused_computation.150 | convolution fusion | flops 5167382528 | bytes 14483456 | tf_op jit(solution)/shard_map/rd,gfd->rgf/dot_general | solution.py:190
  326.8 6.9 %add_convert_fusion = bf16[896,2048]{1,0:T(8,128)(2,1)} fusion(bf16[896,2048]{1,0:T(8,128)(2,1)S(1)} %fusion.44, bf16[704,2048]{1,0:T(8,128)(2,1)} %collective-permute-done.9, f32[896,2,704]{0,2,1:T(8,128)S(1)} %fusion.90), kind=kOutput, calls=%fused_computation.32 | convolution fusion | flops 2596651008 | bytes 15269888 | tf_op jit(solution)/shard_map/dot_general | solution.py:192
  333.6 5.8 reshape.327
  339.5 4.1 all-to-all-start.2
  344.7 92.8 %all-to-all-done.2 = bf16[32,28,2048]{2,1,0:T(8,128)(2,1)} async-done(((bf16[32,28,2048]{2,1,0:T(8,128)(2,1)}), bf16[32,28,2048]{2,1,0:T(8,128)(2,1)}, u32[]{:S(2)}, u32[]{:S(2)}) %all-to-all-start.2) | async-done | bytes 3670048 | tf_op jit(solution)/shard_map/all_to_all | solution.py:196
  437.5 5.8 reshape.328
  443.3 3.9 fusion.40
  448.1 117.0 %all-reduce.5.cloned.1.call-done = bf16[16,2048]{1,0:T(8,128)(2,1)} async-done(((bf16[16,2048]{1,0:T(8,128)(2,1)}), bf16[16,2048]{1,0:T(8,128)(2,1)}) %all-reduce.5.cloned.1.call-update) | async-done | bytes 65552 | tf_op jit(solution)/shard_map/psum | solution.py:217
  566.1 8.4 %fusion.89 = (f32[16]{0:T(128)S(1)}, f32[16,3200]{1,0:T(8,128)S(1)}) fusion(bf16[3200,2048]{1,0:T(8,128)(2,1)} %param.27, bf16[16,2048]{1,0:T(8,128)(2,1)} %all-reduce.5.cloned.1.call-done, f32[2048]{0:T(1024)S(1)} %copy-done.12, f32[16]{0:T(128)S(1)} %add_rsqrt_fusion), kind=kOutput, calls=%fused_computation.149 | convolution fusion | flops 209897456 | bytes 13385856 | tf_op jit(solution)/shard_map/dot_general | solution.py:219
  575.2 40.8 %all-reduce.2 = (f32[512]{0:T(512)S(1)}, f32[512]{0:T(512)S(1)}) all-reduce(f32[512]{0:T(512)S(1)} %dynamic-update-slice, f32[512]{0:T(512)S(1)} %dynamic-update-slice.1), channel_id=2, replica_groups=mesh['seq'=8,'exp'=4] {'seq','exp'}, use_global_device_ids=true, to_apply=%add | all-reduce | flops 1024 | bytes 8192
  616.3 1.3 while.23
  (148 shorter events, 19.6 us)
Async XLA Ops:
  7.2 336.7 %copy-start = (bf16[2048,16]{0,1:T(8,128)(2,1)S(1)}, bf16[2048,16]{0,1:T(8,128)(2,1)}, u32[]{:S(2)}) copy-start(bf16[2048,16]{0,1:T(8,128)(2,1)} %param.22) | copy-start | bytes 196612
  7.2 133.8 %all-gather.4.cloned.1.call-start = ((), (), s32[]{:S(2)}) async-start(), calls=%async_computation.3 | async-start | bytes 4718592 | tf_op jit(solution)/shard_map/all_gather | solution.py:100
  12.4 22.4 %collective-permute-start = (bf16[2,64,2048]{2,1,0:T(8,128)(2,1)}, bf16[2,64,2048]{2,1,0:T(8,128)(2,1)}, u32[]{:S(2)}, u32[]{:S(2)}) collective-permute-start(bf16[2,64,2048]{2,1,0:T(8,128)(2,1)} %constant_dynamic-slice_fusion.2), channel_id=1, source_target_pairs={{0,4},{4,8},{8,12},{12,16},{16,20},{20,24},{24,28},{28,0},{1,5},{5... | collective-permute-start | bytes 1572872 | tf_op jit(solution)/shard_map/ppermute | solution.py:142
  34.9 24.0 %collective-permute-start.1 = (bf16[2,64,2048]{2,1,0:T(8,128)(2,1)}, bf16[2,64,2048]{2,1,0:T(8,128)(2,1)}, u32[]{:S(2)}, u32[]{:S(2)}) collective-permute-start(bf16[2,64,2048]{2,1,0:T(8,128)(2,1)} %collective-permute-done), channel_id=1, source_target_pairs={{0,4},{4,8},{8,12},{12,16},{16,20},{20,24},{24,28},{28,0},{1,5},{5... | collective-permute-start | bytes 1572872 | tf_op jit(solution)/shard_map/ppermute | solution.py:142
  35.0 24.0 %collective-permute-start.4 = (bf16[2,64,2048]{2,1,0:T(8,128)(2,1)}, bf16[2,64,2048]{2,1,0:T(8,128)(2,1)}, u32[]{:S(2)}, u32[]{:S(2)}) collective-permute-start(bf16[2,64,2048]{2,1,0:T(8,128)(2,1)} %constant_dynamic-slice_fusion.2), channel_id=1, source_target_pairs={{4,0},{8,4},{12,8},{16,12},{20,16},{24,20},{28,24},{0,28},{5,1},{9... | collective-permute-start | bytes 1572872 | tf_op jit(solution)/shard_map/ppermute | solution.py:144
  47.2 11.6 %copy-start.14 = (s32[1,4]{1,0:T(1,128)S(1)}, s32[1,4]{1,0:T(1,128)}, u32[]{:S(2)}) copy-start(s32[1,4]{1,0:T(1,128)} %param.17) | copy-start | bytes 52
  50.2 81.2 %copy-start.7 = (bf16[2,128,2048]{2,1,0:T(8,128)(2,1)S(1)}, bf16[2,128,2048]{2,1,0:T(8,128)(2,1)}, u32[]{:S(2)}) copy-start(bf16[2,128,2048]{2,1,0:T(8,128)(2,1)} %param.20) | copy-start | bytes 3145732
  58.8 33.7 %collective-permute-start.2 = (bf16[2,64,2048]{2,1,0:T(8,128)(2,1)}, bf16[2,64,2048]{2,1,0:T(8,128)(2,1)S(1)}, u32[]{:S(2)}, u32[]{:S(2)}) collective-permute-start(bf16[2,64,2048]{2,1,0:T(8,128)(2,1)} %collective-permute-done.1), channel_id=1, source_target_pairs={{0,4},{4,8},{8,12},{12,16},{16,20},{20,24},{24,28},{28,0},{1,5},{5... | collective-permute-start | bytes 1572872 | tf_op jit(solution)/shard_map/ppermute | solution.py:142
  59.0 37.7 %collective-permute-start.5 = (bf16[2,64,2048]{2,1,0:T(8,128)(2,1)}, bf16[2,64,2048]{2,1,0:T(8,128)(2,1)S(1)}, u32[]{:S(2)}, u32[]{:S(2)}) collective-permute-start(bf16[2,64,2048]{2,1,0:T(8,128)(2,1)} %collective-permute-done.4), channel_id=1, source_target_pairs={{4,0},{8,4},{12,8},{16,12},{20,16},{24,20},{28,24},{0,28},{5,1},{9... | collective-permute-start | bytes 1572872 | tf_op jit(solution)/shard_map/ppermute | solution.py:144
  92.5 33.3 %collective-permute-start.3 = (bf16[2,64,2048]{2,1,0:T(8,128)(2,1)S(1)}, bf16[2,64,2048]{2,1,0:T(8,128)(2,1)S(1)}, u32[]{:S(2)}, u32[]{:S(2)}) collective-permute-start(bf16[2,64,2048]{2,1,0:T(8,128)(2,1)S(1)} %collective-permute-done.2), channel_id=1, source_target_pairs={{0,4},{4,8},{8,12},{12,16},{16,20},{20,24},{24,28},{28,0},{1,5},{5... | collective-permute-start | bytes 1572872 | tf_op jit(solution)/shard_map/ppermute | solution.py:142
  96.7 38.3 %collective-permute-start.6 = (bf16[2,64,2048]{2,1,0:T(8,128)(2,1)S(1)}, bf16[2,64,2048]{2,1,0:T(8,128)(2,1)S(1)}, u32[]{:S(2)}, u32[]{:S(2)}) collective-permute-start(bf16[2,64,2048]{2,1,0:T(8,128)(2,1)S(1)} %collective-permute-done.5), channel_id=1, source_target_pairs={{4,0},{8,4},{12,8},{16,12},{20,16},{24,20},{28,24},{0,28},{5,1},{9... | collective-permute-start | bytes 1572872 | tf_op jit(solution)/shard_map/ppermute | solution.py:144
  135.9 5.1 copy-start.4
  141.0 47.7 %collective-permute-start.7 = (bf16[16,64,2048]{2,1,0:T(8,128)(2,1)}, bf16[16,64,2048]{2,1,0:T(8,128)(2,1)}, u32[]{:S(2)}, u32[]{:S(2)}) collective-permute-start(bf16[16,64,2048]{2,1,0:T(8,128)(2,1)} %bitcast.153), channel_id=1, source_target_pairs={{0,1},{1,0},{2,3},{3,2},{4,5},{5,4},{6,7},{7,6},{8,9},{9,8},{10,11... | collective-permute-start | bytes 12582920 | tf_op jit(solution)/shard_map/ppermute | solution.py:60
  146.3 1.0 copy-start.6
  146.5 1.7 copy-start.8
  148.2 25.0 %copy-start.11 = (s32[1,128,6]{1,0,2:T(1,128)S(1)}, s32[1,128,6]{1,0,2:T(1,128)}, u32[]{:S(2)}) copy-start(s32[1,128,6]{1,0,2:T(1,128)} %param.23) | copy-start | bytes 9220
  167.1 24.6 %copy-start.2 = (bf16[1,128,2048]{2,1,0:T(8,128)(2,1)S(1)}, bf16[1,128,2048]{2,1,0:T(8,128)(2,1)}, u32[]{:S(2)}) copy-start(bf16[1,128,2048]{2,1,0:T(8,128)(2,1)} %param.16) | copy-start | bytes 1572868
  167.1 21.3 %all-to-all-start = ((bf16[8,128,256]{2,1,0:T(8,128)(2,1)}), bf16[8,128,256]{2,1,0:T(8,128)(2,1)S(1)}, u32[]{:S(2)}, u32[]{:S(2)}) async-start(bf16[8,128,256]{2,1,0:T(8,128)(2,1)} %all_to_all.18), calls=%async_computation | async-start | bytes 1048576 | tf_op jit(solution)/shard_map/all_to_all | solution.py:132
  188.6 3.5 copy-start.1
  192.1 0.9 copy-start.10
  201.8 97.7 %all-to-all-start.1 = ((bf16[32,28,2048]{2,1,0:T(8,128)(2,1)}), bf16[32,28,2048]{2,1,0:T(8,128)(2,1)}, u32[]{:S(2)}, u32[]{:S(2)}) async-start(bf16[32,28,2048]{2,1,0:T(8,128)(2,1)} %reshape.325), calls=%async_computation.1 | async-start | bytes 8388608 | tf_op jit(solution)/shard_map/all_to_all | solution.py:185
  205.7 112.7 %collective-permute-start.8 = (bf16[2,704,2048]{2,1,0:T(8,128)(2,1)}, bf16[2,704,2048]{2,1,0:T(8,128)(2,1)}, u32[]{:S(2)}, u32[]{:S(2)}) collective-permute-start(bf16[2,704,2048]{2,1,0:T(8,128)(2,1)} %bitcast.164), channel_id=1, source_target_pairs={{0,1},{1,0},{2,3},{3,2},{4,5},{5,4},{6,7},{7,6},{8,9},{9,8},{10,11... | collective-permute-start | bytes 17301512 | tf_op jit(solution)/shard_map/ppermute | solution.py:60
  205.9 120.9 %collective-permute-start.9 = (bf16[704,2048]{1,0:T(8,128)(2,1)}, bf16[704,2048]{1,0:T(8,128)(2,1)}, u32[]{:S(2)}, u32[]{:S(2)}) collective-permute-start(bf16[704,2048]{1,0:T(8,128)(2,1)} %bitcast.165), channel_id=1, source_target_pairs={{0,1},{1,0},{2,3},{3,2},{4,5},{5,4},{6,7},{7,6},{8,9},{9,8},{10,11... | collective-permute-start | bytes 8650760 | tf_op jit(solution)/shard_map/ppermute | solution.py:60
  305.5 9.4 %copy-start.13 = (bf16[1,704,2048]{2,1,0:T(8,128)(2,1)S(1)}, bf16[1,704,2048]{2,1,0:T(8,128)(2,1)}, u32[]{:S(2)}) copy-start(bf16[1,704,2048]{2,1,0:T(8,128)(2,1)} %param.25) | copy-start | bytes 8650756
  314.9 3.4 copy-start.3
  339.5 98.0 %all-to-all-start.2 = ((bf16[32,28,2048]{2,1,0:T(8,128)(2,1)}), bf16[32,28,2048]{2,1,0:T(8,128)(2,1)}, u32[]{:S(2)}, u32[]{:S(2)}) async-start(bf16[32,28,2048]{2,1,0:T(8,128)(2,1)} %reshape.327), calls=%async_computation.2 | async-start | bytes 8388608 | tf_op jit(solution)/shard_map/all_to_all | solution.py:196
  343.6 221.6 %all-reduce.5.cloned.1.call-start = ((), (), s32[]{:S(2)}) async-start(), calls=%async_computation.4 | async-start | bytes 131072 | tf_op jit(solution)/shard_map/psum | solution.py:217
  443.3 122.8 %copy-start.12 = (f32[2048]{0:T(1024)S(1)}, f32[2048]{0:T(1024)}, u32[]{:S(2)}) copy-start(f32[2048]{0:T(1024)} %param.26) | copy-start | bytes 24580
  447.2 127.3 %copy-start.5 = (bf16[128,2048]{1,0:T(8,128)(2,1)}, bf16[128,2048]{1,0:T(8,128)(2,1)S(1)}, u32[]{:S(2)}) copy-start(bf16[128,2048]{1,0:T(8,128)(2,1)S(1)} %fusion.40) | copy-start | bytes 1572868
  447.4 0.6 copy-start.9
Sparse Core Ops, SparseCore 0:
  10.6 129.3 all-gather.3
  448.2 116.8 all-reduce.4
